TPU v7x, 32 devices: a whole 2x2x4 slice. The times are simulated.
32 devices in a mesh: dom: 2 (over y), blk: 16 (over z, x, core).
Axes of the slice: x: 2, y: 2, z: 4, core: 2. Of those that a mesh axis runs over, the one named last changes fastest.
Arguments:
- right_side: float32 [2, 4, 2, 8192], P(None, None, 'dom', 'blk')
- near_blocks: bfloat16 [2, 32, 4, 2, 256, 256], P('dom', 'blk'), may hold values from -0.125 to 0.125
- near_cols: int32 [2, 32, 4], P('dom', 'blk'), may hold values from 0 to 5
- partner: int32 [2, 32], P('dom', 'blk'), may hold values from 0 to 3, as said below
- source_basis: bfloat16 [2, 2, 64, 8192], P('dom', None, None, 'blk'), may hold values from -0.25 to 0.25
- target_basis: bfloat16 [2, 2, 64, 8192], P('dom', None, None, 'blk'), may hold values from -0.75 to 0.75
- coupling: float32 [2, 16, 16, 2, 64, 64], P('dom', 'blk'), as said below
- far_ranks: int32 [2, 16, 16], P('dom', 'blk'), may hold values from 32 to 64, as said below
Outputs:
- second_basis: float32 [2, 4, 2, 8192], P(None, None, 'dom', 'blk')
- third_basis: float32 [2, 4, 2, 8192], P(None, None, 'dom', 'blk')
- hessenberg: float32 [4, 9], replicated
Inputs may be any that keep to these rules, and one draw needn't show every extreme that they name: partner[d, c * 2 + i] = e * 2 + j names block j of cluster c in subdomain e; the named block names the first one back, and no block names itself. coupling[d, c, s, a, k, l] equals coupling[d, s, c, a, l, k]. far_ranks[d, c, s] equals far_ranks[d, s, c].
All inputs are finite; a program needn't handle non-finite values.
Results may differ from a plain program's by a relative error of at most 0.0065.
Values may be sent and summed in bfloat16 or wider, within the bound.
No kernel may reach another device: no remote copies, remote signals or barrier semaphores. Data moves between devices by JAX's collectives and lax.ppermute only.
A program may use at most 64 MiB of HBM per device.

v0:
```python
import jax
import jax.numpy as jnp
from jax import lax
from jax.sharding import PartitionSpec as P

EPSILON = 1e-06


def extended(cells, sides, width):
    for axis, dim in sides:
        count = lax.axis_size(axis)
        ends = count - 1
        head = lax.slice_in_dim(cells, 0, width, axis=dim)
        tail = lax.slice_in_dim(cells, cells.shape[dim] - width, cells.shape[dim], axis=dim)
        cells = jnp.concatenate(
            [
                lax.ppermute(tail, axis, [(i, (i + 1) % count) for i in range(ends)]),
                cells,
                lax.ppermute(head, axis, [((i + 1) % count, i) for i in range(ends)]),
            ],
            axis=dim,
        )
    return cells


def complex_mix(products):
    return jnp.stack([products[0, 0] - products[1, 1], products[0, 1] + products[1, 0]])


def apply_operator(
    vector, near_blocks, near_cols, partner, source_basis, target_basis, coupling, far_ranks
):
    nrhs = vector.shape[1]
    rows = vector.shape[3]
    blocks_dev = near_blocks.shape[1]
    slots = near_blocks.shape[2]
    width = near_blocks.shape[4]
    rank_cap = source_basis.shape[2]
    rounded = vector.astype(jnp.bfloat16)
    window = extended(rounded, (("blk", 3),), rows)
    window = window.reshape(2, nrhs, 3 * blocks_dev, width)
    chosen = jnp.take(window, near_cols[0].reshape(-1), axis=2).reshape(
        2, nrhs, blocks_dev, slots, width
    )
    near_prod = jnp.einsum(
        "ikarc,pqikc->apqir", near_blocks[0], chosen, preferred_element_type=jnp.float32
    )
    near_part = complex_mix(near_prod).reshape(2, nrhs, 1, rows)
    coef_prod = jnp.einsum(
        "akr,pqr->apqk", source_basis[0], rounded[:, :, 0], preferred_element_type=jnp.float32
    )
    coeffs = jnp.stack([coef_prod[0, 0] + coef_prod[1, 1], coef_prod[0, 1] - coef_prod[1, 0]])
    row_coupling = coupling[0, 0]
    row_ranks = far_ranks[0, 0]
    levels = jnp.arange(rank_cap, dtype=jnp.int32)
    limit = row_ranks[:, None, None]
    keep = (levels[None, :, None] < limit) & (levels[None, None, :] < limit)
    weights = row_coupling * keep[:, None].astype(jnp.float32)
    inner = jnp.einsum(
        "sakl,spql->apqk",
        weights,
        lax.all_gather(coeffs[None], "blk", axis=0, tiled=True),
        precision=lax.Precision.HIGHEST,
    )
    far_coef = complex_mix(inner)
    rounded_coef = far_coef.astype(jnp.bfloat16)
    outward = jnp.einsum(
        "akr,pqk->apqr", target_basis[0], rounded_coef, preferred_element_type=jnp.float32
    )
    far_part = complex_mix(outward).reshape(2, nrhs, 1, rows)
    every = lax.all_gather(vector, "dom", axis=2, tiled=True)
    every = every.reshape(2, nrhs, -1, width)
    mates = jnp.take(every, partner[0], axis=2).reshape(2, nrhs, 1, rows)
    return vector + near_part + far_part - mates


def local_products(vectors, image):
    stacked = []
    for basis in vectors:
        real_part = jnp.sum(basis[0] * image[0] + basis[1] * image[1], axis=(1, 2))
        imag_part = jnp.sum(basis[0] * image[1] - basis[1] * image[0], axis=(1, 2))
        stacked.append(jnp.stack([real_part, imag_part]))
    return jnp.stack(stacked)


def local_squares(field):
    return jnp.sum(field[0] * field[0] + field[1] * field[1], axis=(1, 2))


def scaled(factor, field):
    real_f = factor[0][:, None, None]
    imag_f = factor[1][:, None, None]
    return jnp.stack([real_f * field[0] - imag_f * field[1], real_f * field[1] + imag_f * field[0]])


def shards(
    right_side, near_blocks, near_cols, partner, source_basis, target_basis, coupling, far_ranks
):
    rows = right_side.shape[3]
    total = float(rows * lax.axis_size("dom") * lax.axis_size("blk"))

    def operator(field):
        return apply_operator(
            field, near_blocks, near_cols, partner, source_basis, target_basis, coupling, far_ranks
        )

    start_sum = lax.psum(local_squares(right_side), ("dom", "blk"))
    beta = jnp.sqrt(start_sum / total + EPSILON)
    first_vec = right_side / beta[None, :, None, None]
    image_one = operator(first_vec)

    def projections(vectors, image):
        return lax.psum(local_products(vectors, image), ("dom", "blk")) / total

    def lengths(field):
        return lax.psum(local_squares(field), ("dom", "blk")) / total

    h_one_one = projections([first_vec], image_one)[0]
    rest_one = image_one - scaled(h_one_one, first_vec)
    h_two_one = jnp.sqrt(lengths(rest_one) + EPSILON)
    second_basis = rest_one / h_two_one[None, :, None, None]
    image_two = operator(second_basis)
    both = projections([first_vec, second_basis], image_two)
    h_one_two = both[0]
    h_two_two = both[1]
    rest_two = image_two - scaled(h_one_two, first_vec) - scaled(h_two_two, second_basis)
    h_three_two = jnp.sqrt(lengths(rest_two) + EPSILON)
    third_basis = rest_two / h_three_two[None, :, None, None]
    hessenberg = jnp.stack(
        [
            beta,
            h_one_one[0],
            h_one_one[1],
            h_two_one,
            h_one_two[0],
            h_one_two[1],
            h_two_two[0],
            h_two_two[1],
            h_three_two,
        ],
        axis=1,
    )
    return (second_basis, third_basis, hessenberg)


def solution(mesh):
    return jax.shard_map(
        shards,
        mesh=mesh,
        in_specs=(
            P(None, None, "dom", "blk"),
            P("dom", "blk", None, None, None, None),
            P("dom", "blk", None),
            P("dom", "blk"),
            P("dom", None, None, "blk"),
            P("dom", None, None, "blk"),
            P("dom", "blk", None, None, None, None),
            P("dom", "blk", None),
        ),
        out_specs=(P(None, None, "dom", "blk"), P(None, None, "dom", "blk"), P()),
        check_vma=False,
    )
```

profile of v0, /device:TPU:0, one launch (start us, length us, event | category | flops | bytes accessed | tf_op | source)
XLA Modules:
  0.0 278.6 jit_solution(17837477689193010791)
XLA Ops:
  0.6 0.0 copy-start
  0.6 0.0 copy-start.2
  0.7 0.0 copy-start.3
  0.7 0.0 copy-start.4
  0.7 1.0 add_reduce_fusion.3
  1.7 42.0 %psum.35 = f32[4]{0:T(128)S(1)} all-reduce(f32[4]{0:T(128)S(1)} %add_reduce_fusion.3), channel_id=1, replica_groups=mesh['dom'=2,'blk'=16] {'dom','blk'}, use_global_device_ids=true, to_apply=%region_1.0 | all-reduce | flops 4 | bytes 32 | tf_op jit(solution)/shard_map/psum | solution.py:107
  43.7 0.8 fusion.64
  44.5 1.3 collective-permute-start
  45.8 1.3 collective-permute-start.1
  47.1 1.1 convolution_bitcast_fusion.3
  48.2 24.1 %all-gather = f32[32,4,64]{2,1,0:T(4,128)S(1)} all-gather(f32[2,4,64]{2,1,0:T(4,128)S(1)} %pad_maximum_fusion.2), channel_id=2, replica_groups=mesh['dom'=2,'blk'=16] {'blk'}, dimensions={0}, use_global_device_ids=true | all-gather | bytes 34816 | tf_op jit(solution)/shard_map/all_gather | solution.py:62
  72.3 0.7 iota_compare_fusion
  73.0 0.2 and_convert_fusion
  73.2 2.6 fusion.12
  75.9 0.0 copy-start.1
  75.9 0.1 convolution_bitcast_fusion.1
  76.1 0.1 reshape_squeeze.4
  76.2 4.4 %all_gather.13 = f32[2,4,2,512]{3,1,0,2:T(4,128)S(1)} all-gather(f32[2,4,1,512]{3,1,0,2:T(4,128)S(1)} %get-tuple-element.28), channel_id=1, replica_groups=mesh['dom'=2,'blk'=16] {'dom'}, dimensions={2}, use_global_device_ids=true | all-gather | bytes 49152 | tf_op jit(solution)/shard_map/all_gather | solution.py:71
  80.7 0.6 gather_fusion.1
  81.3 0.1 select_bitcast_fusion.1
  81.5 0.0 collective-permute-done
  81.5 0.0 collective-permute-done.1
  81.5 0.6 gather_fusion
  82.1 0.1 broadcast_select_fusion.1
  82.2 0.7 fusion.4
  82.9 0.1 add_reduce_fusion.2
  83.1 36.9 %psum.36 = f32[1,2,4]{2,1,0:T(2,128)S(1)} all-reduce(f32[1,2,4]{2,1,0:T(2,128)S(1)} %maximum_bitcast_fusion.6), channel_id=1, replica_groups=mesh['dom'=2,'blk'=16] {'dom','blk'}, use_global_device_ids=true, to_apply=%region_4.7 | all-reduce | flops 8 | bytes 64 | tf_op jit(solution)/shard_map/psum | solution.py:113
  120.0 0.1 multiply_subtract_fusion.2
  120.1 0.1 fusion.34
  120.2 0.1 copy.136
  120.3 41.3 %psum.37 = f32[4]{0:T(128)S(1)} all-reduce(f32[4]{0:T(128)S(1)} %fusion.34), channel_id=1, replica_groups=mesh['dom'=2,'blk'=16] {'dom','blk'}, use_global_device_ids=true, to_apply=%region_6.9 | all-reduce | flops 4 | bytes 32 | tf_op jit(solution)/shard_map/psum | solution.py:116
  161.6 0.1 fusion.63
  161.7 0.1 convolution_bitcast_fusion.2
  161.9 20.6 %all-gather.1 = f32[32,4,64]{2,1,0:T(4,128)S(1)} all-gather(f32[2,4,64]{2,1,0:T(4,128)S(1)} %pad_maximum_fusion.3), channel_id=3, replica_groups=mesh['dom'=2,'blk'=16] {'blk'}, dimensions={0}, use_global_device_ids=true | all-gather | bytes 34816 | tf_op jit(solution)/shard_map/all_gather | solution.py:62
  182.5 2.6 fusion.10
  185.1 2.2 collective-permute-start.2
  187.4 1.3 collective-permute-start.3
  188.7 4.4 %all_gather.15 = f32[2,4,2,512]{3,1,0,2:T(4,128)S(1)} all-gather(f32[2,4,1,512]{3,1,0,2:T(4,128)S(1)} %get-tuple-element.26), channel_id=1, replica_groups=mesh['dom'=2,'blk'=16] {'dom'}, dimensions={2}, use_global_device_ids=true | all-gather | bytes 49152 | tf_op jit(solution)/shard_map/all_gather | solution.py:71
  193.2 0.6 gather_fusion.3
  193.8 0.1 select_bitcast_fusion
  193.9 0.1 convolution_bitcast_fusion
  194.0 0.6 copy.145
  194.7 0.1 copy.139
  194.8 0.0 collective-permute-done.2
  194.8 0.0 collective-permute-done.3
  194.8 0.6 gather_fusion.2
  195.4 0.1 broadcast_select_fusion
  195.5 0.7 fusion.7
  196.2 0.2 add_reduce_fusion.1
  196.4 0.1 copy.137
  196.5 39.3 %psum.38 = f32[2,2,4]{2,1,0:T(2,128)S(1)} all-reduce(f32[2,2,4]{2,1,0:T(2,128)S(1)} %pad_maximum_fusion.4), channel_id=1, replica_groups=mesh['dom'=2,'blk'=16] {'dom','blk'}, use_global_device_ids=true, to_apply=%region_11.14 | all-reduce | flops 16 | bytes 128 | tf_op jit(solution)/shard_map/psum | solution.py:113
  235.8 0.1 multiply_subtract_fusion
  235.9 0.1 multiply_subtract_fusion.1
  236.0 0.1 fusion.30
  236.1 0.1 copy.138
  236.2 40.5 %psum.39 = f32[4]{0:T(128)S(1)} all-reduce(f32[4]{0:T(128)S(1)} %fusion.30), channel_id=1, replica_groups=mesh['dom'=2,'blk'=16] {'dom','blk'}, use_global_device_ids=true, to_apply=%region_13.16 | all-reduce | flops 4 | bytes 32 | tf_op jit(solution)/shard_map/psum | solution.py:116
  276.7 0.1 copy.144
  276.8 0.1 copy.140
  276.9 0.1 copy.141
  277.0 0.1 copy.142
  277.1 0.1 copy.143
  277.2 0.1 broadcast_divide_fusion
  277.3 0.6 copy.146
  277.9 0.7 stack.135
  (56 shorter events, 0.5 us)
Async XLA Ops:
  0.6 81.5 %copy-start = (bf16[1,2,4,2,256,256]{5,4,3,2,1,0:T(8,128)(2,1)S(1)}, bf16[1,2,4,2,256,256]{5,4,3,2,1,0:T(8,128)(2,1)}, u32[]{:S(2)}) copy-start(bf16[1,2,4,2,256,256]{5,4,3,2,1,0:T(8,128)(2,1)} %param.13) | copy-start | bytes 6291460
  0.6 75.3 %copy-start.2 = (bf16[1,2,64,512]{3,2,1,0:T(8,128)(2,1)S(1)}, bf16[1,2,64,512]{3,2,1,0:T(8,128)(2,1)}, u32[]{:S(2)}) copy-start(bf16[1,2,64,512]{3,2,1,0:T(8,128)(2,1)} %param.17) | copy-start | bytes 393220
  0.7 75.4 %copy-start.3 = (s32[1,2,4]{2,1,0:T(2,128)S(1)}, s32[1,2,4]{2,1,0:T(2,128)}, u32[]{:S(2)}) copy-start(s32[1,2,4]{2,1,0:T(2,128)} %param.14) | copy-start | bytes 100
  0.7 75.5 %copy-start.4 = (s32[1,2]{1,0:T(1,128)S(1)}, s32[1,2]{1,0:T(1,128)}, u32[]{:S(2)}) copy-start(s32[1,2]{1,0:T(1,128)} %param.15) | copy-start | bytes 28
  44.5 37.0 %collective-permute-start = (bf16[2,4,1,512]{3,1,0,2:T(4,128)(2,1)S(1)}, bf16[2,4,1,512]{3,1,0,2:T(4,128)(2,1)S(1)}, u32[]{:S(2)}, u32[]{:S(2)}) collective-permute-start(bf16[2,4,1,512]{3,1,0,2:T(4,128)(2,1)S(1)} %get-tuple-element.27), channel_id=1, source_target_pairs={{0,1},{1,2},{2,3},{3,4},{4,5},{5,6},{6,7},{7,8},{8,9},{9,10},{10,1... | collective-permute-start | bytes 24584 | tf_op jit(solution)/shard_map/ppermute | solution.py:17
  45.8 35.7 %collective-permute-start.1 = (bf16[2,4,1,512]{3,1,0,2:T(4,128)(2,1)S(1)}, bf16[2,4,1,512]{3,1,0,2:T(4,128)(2,1)S(1)}, u32[]{:S(2)}, u32[]{:S(2)}) collective-permute-start(bf16[2,4,1,512]{3,1,0,2:T(4,128)(2,1)S(1)} %get-tuple-element.27), channel_id=1, source_target_pairs={{1,0},{2,1},{3,2},{4,3},{5,4},{6,5},{7,6},{8,7},{9,8},{10,9},{11,1... | collective-permute-start | bytes 24584 | tf_op jit(solution)/shard_map/ppermute | solution.py:19
  75.9 85.8 %copy-start.1 = (bf16[1,2,64,512]{3,2,1,0:T(8,128)(2,1)S(1)}, bf16[1,2,64,512]{3,2,1,0:T(8,128)(2,1)}, u32[]{:S(2)}) copy-start(bf16[1,2,64,512]{3,2,1,0:T(8,128)(2,1)} %param.16) | copy-start | bytes 393220
  185.1 9.7 %collective-permute-start.2 = (bf16[2,4,1,512]{3,1,0,2:T(4,128)(2,1)S(1)}, bf16[2,4,1,512]{3,1,0,2:T(4,128)(2,1)S(1)}, u32[]{:S(2)}, u32[]{:S(2)}) collective-permute-start(bf16[2,4,1,512]{3,1,0,2:T(4,128)(2,1)S(1)} %get-tuple-element.25), channel_id=1, source_target_pairs={{0,1},{1,2},{2,3},{3,4},{4,5},{5,6},{6,7},{7,8},{8,9},{9,10},{10,1... | collective-permute-start | bytes 24584 | tf_op jit(solution)/shard_map/ppermute | solution.py:17
  187.4 7.4 %collective-permute-start.3 = (bf16[2,4,1,512]{3,1,0,2:T(4,128)(2,1)S(1)}, bf16[2,4,1,512]{3,1,0,2:T(4,128)(2,1)S(1)}, u32[]{:S(2)}, u32[]{:S(2)}) collective-permute-start(bf16[2,4,1,512]{3,1,0,2:T(4,128)(2,1)S(1)} %get-tuple-element.25), channel_id=1, source_target_pairs={{1,0},{2,1},{3,2},{4,3},{5,4},{6,5},{7,6},{8,7},{9,8},{10,9},{11,1... | collective-permute-start | bytes 24584 | tf_op jit(solution)/shard_map/ppermute | solution.py:19
where the time goes:
time: 280 us; the launch traced here: 279 us
  blocking collectives  254 us (91%)
  matrix products  8.05 us (3%)
  starting transfers between devices  6.11 us (2%)
  local copies, waits for them, and re-layouts  5.44 us (2%)
  other arithmetic  4.26 us (2%)
    psum x2, blocking collectives, lengths(): return lax.psum(local_squares(field), ('dom', 'blk')) / total  81.9 us
    psum x2, blocking collectives, projections(): return lax.psum(local_products(vectors, image), ('dom', 'blk')) / total  76.2 us
    all_gather x2, blocking collectives, apply_operator(): lax.all_gather(coeffs[None], 'blk', axis=0, tiled=True)  44.7 us
    psum x1, blocking collectives, shards(): start_sum = lax.psum(local_squares(right_side), ('dom', 'blk'))  42 us
    all_gather x2, blocking collectives, apply_operator(): every = lax.all_gather(vector, 'dom', axis=2, tiled=True)  8.85 us
  transfers between devices with their start and end apart: 4, of which 0 were waited for; matrix products, arithmetic and copies ran while one was open for 3% of the time, Pallas kernels for 0%

commit v1 on v0

--- a/solution.py
+++ b/solution.py
@@ -4,6 +4,22 @@
 from jax.sharding import PartitionSpec as P
 
 EPSILON = 1e-06
+
+
+def product_in_turn(value, axis, dim, term):
+    devices, here, rows = (lax.axis_size(axis), lax.axis_index(axis), value.shape[dim])
+    upward = [(i, (i + 1) % devices) for i in range(devices)]
+    downward = [(i, (i - 1) % devices) for i in range(devices)]
+    half = devices // 2
+    from_left = from_right = value
+    running = term(value, here * rows)
+    for step in range(1, half + 1):
+        from_left = lax.ppermute(from_left, axis, upward)
+        if step < devices - half:
+            from_right = lax.ppermute(from_right, axis, downward)
+            running = running + term(from_right, (here + step) % devices * rows)
+        running = running + term(from_left, (here - step) % devices * rows)
+    return running
 
 
 def extended(cells, sides, width):
@@ -56,11 +72,16 @@
     limit = row_ranks[:, None, None]
     keep = (levels[None, :, None] < limit) & (levels[None, None, :] < limit)
     weights = row_coupling * keep[:, None].astype(jnp.float32)
-    inner = jnp.einsum(
-        "sakl,spql->apqk",
-        weights,
-        lax.all_gather(coeffs[None], "blk", axis=0, tiled=True),
-        precision=lax.Precision.HIGHEST,
+    inner = product_in_turn(
+        coeffs[None],
+        "blk",
+        0,
+        lambda shard, start: jnp.einsum(
+            "sakl,spql->apqk",
+            lax.dynamic_slice_in_dim(weights, start, shard.shape[0], axis=0),
+            shard,
+            precision=lax.Precision.HIGHEST,
+        ),
     )
     far_coef = complex_mix(inner)
     rounded_coef = far_coef.astype(jnp.bfloat16)

time: 280 us -> 326 us (1.16)
  starting transfers between devices: 6.11 us -> 66 us
  blocking collectives: 254 us -> 208 us
  waiting for transfers between devices: 0.01 us -> 24 us
  other arithmetic: 4.26 us -> 7.85 us
    ppermute x0 -> x30, starting transfers between devices: none -> 59.4 us  [the longest x14 58.7 us: product_in_turn(): from_right = lax.ppermute(from_right, axis, downward)]
    all_gather x2 -> x0, blocking collectives: 44.7 us -> none  [apply_operator(): lax.all_gather(coeffs[None], 'blk', axis=0, tiled=True)]
    ppermute x0 -> x30, waiting for transfers between devices: none -> 24 us  [the longest x16 22.5 us: product_in_turn(): from_left = lax.ppermute(from_left, axis, upward)]
    dot_general x2 -> x32, matrix products: 5.25 us -> 8.17 us  [apply_operator(): jnp.einsum('sakl,spql->apqk', lax.dynamic_slice_in_dim(weights, start, sh...]
  transfers between devices with their start and end apart: 4 -> 34, of which waited for: 0 -> 16; matrix products, arithmetic and copies ran while one was open for 3% -> 6% of each run, Pallas kernels for 0% -> 0%
where the time goes in v1:
time: 326 us; the launch traced here: 325 us
  blocking collectives  208 us (64%)
  starting transfers between devices  66 us (20%)
  waiting for transfers between devices  24 us (7%)
  matrix products  11 us (3%)
  other arithmetic  7.85 us (2%)
  local copies, waits for them, and re-layouts  6.14 us (2%)
    psum x2, blocking collectives, lengths(): return lax.psum(local_squares(field), ('dom', 'blk')) / total  83.6 us
    psum x2, blocking collectives, projections(): return lax.psum(local_products(vectors, image), ('dom', 'blk')) / total  73.7 us
    ppermute x14, starting transfers between devices, product_in_turn(): from_right = lax.ppermute(from_right, axis, downward)  58.7 us
    psum x1, blocking collectives, shards(): start_sum = lax.psum(local_squares(right_side), ('dom', 'blk'))  42 us
    ppermute x16, waiting for transfers between devices, product_in_turn(): from_left = lax.ppermute(from_left, axis, upward)  22.5 us
    all_gather x2, blocking collectives, apply_operator(): every = lax.all_gather(vector, 'dom', axis=2, tiled=True)  8.82 us
    dot_general x32, matrix products, apply_operator(): jnp.einsum('sakl,spql->apqk', lax.dynamic_slice_in_dim(weights, start, sh...  8.17 us
  transfers between devices with their start and end apart: 34, of which 16 were waited for; matrix products, arithmetic and copies ran while one was open for 6% of the time, Pallas kernels for 0%

profile of v1, /device:TPU:0, one launch (start us, length us, event | category | flops | bytes accessed | tf_op | source)
XLA Modules:
  0.0 324.9 jit_solution(12209842988067755331)
XLA Ops:
  0.6 1.0 add_reduce_fusion.3
  1.6 42.0 %psum.35 = f32[4]{0:T(128)S(1)} all-reduce(f32[4]{0:T(128)S(1)} %add_reduce_fusion.3), channel_id=1, replica_groups=mesh['dom'=2,'blk'=16] {'dom','blk'}, use_global_device_ids=true, to_apply=%region_1.0 | all-reduce | flops 4 | bytes 32 | tf_op jit(solution)/shard_map/psum | solution.py:128
  43.6 0.8 fusion.218
  44.4 1.1 convolution_bitcast_fusion.3
  45.5 1.7 collective-permute-start.2
  47.2 2.7 collective-permute-start
  50.0 1.3 collective-permute-start.1
  51.5 0.8 reshape_squeeze.4
  52.3 0.7 compare_select_fusion
  52.9 0.7 compare_and_fusion
  53.6 0.7 iota_compare_fusion
  54.3 1.0 and_convert_fusion
  55.3 4.4 %all_gather.6 = f32[2,4,2,512]{3,1,0,2:T(4,128)S(1)} all-gather(f32[2,4,1,512]{3,1,0,2:T(4,128)S(1)} %get-tuple-element.25), channel_id=1, replica_groups=mesh['dom'=2,'blk'=16] {'dom'}, dimensions={2}, use_global_device_ids=true | all-gather | bytes 49152 | tf_op jit(solution)/shard_map/all_gather | solution.py:92
  59.8 1.5 bitcast_multiply_fusion
  61.6 0.6 gather_fusion.1
  62.6 4.3 %collective-permute-start.4 = (f32[1,2,4,64]{3,2,1,0:T(4,128)S(1)}, f32[1,2,4,64]{3,2,1,0:T(4,128)S(1)}, u32[]{:S(2)}, u32[]{:S(2)}) collective-permute-start(f32[1,2,4,64]{3,2,1,0:T(4,128)S(1)} %collective-permute-done.2), channel_id=1, source_target_pairs={{0,15},{1,0},{2,1},{3,2},{4,3},{5,4},{6,5},{7,6},{8,7},{9,8},{10,9... | collective-permute-start | bytes 6152 | tf_op jit(solution)/shard_map/ppermute | solution.py:19
  67.2 0.3 convolution_add_fusion.16
  67.4 0.7 collective-permute-done.5
  68.5 4.5 %collective-permute-start.6 = (f32[1,2,4,64]{3,2,1,0:T(4,128)S(1)}, f32[1,2,4,64]{3,2,1,0:T(4,128)S(1)}, u32[]{:S(2)}, u32[]{:S(2)}) collective-permute-start(f32[1,2,4,64]{3,2,1,0:T(4,128)S(1)} %collective-permute-done.4), channel_id=1, source_target_pairs={{0,15},{1,0},{2,1},{3,2},{4,3},{5,4},{6,5},{7,6},{8,7},{9,8},{10,9... | collective-permute-start | bytes 6152 | tf_op jit(solution)/shard_map/ppermute | solution.py:19
  73.2 0.7 collective-permute-done.7
  74.3 4.4 %collective-permute-start.8 = (f32[1,2,4,64]{3,2,1,0:T(4,128)S(1)}, f32[1,2,4,64]{3,2,1,0:T(4,128)S(1)}, u32[]{:S(2)}, u32[]{:S(2)}) collective-permute-start(f32[1,2,4,64]{3,2,1,0:T(4,128)S(1)} %collective-permute-done.6), channel_id=1, source_target_pairs={{0,15},{1,0},{2,1},{3,2},{4,3},{5,4},{6,5},{7,6},{8,7},{9,8},{10,9... | collective-permute-start | bytes 6152 | tf_op jit(solution)/shard_map/ppermute | solution.py:19
  79.0 0.6 gather_fusion
  79.7 0.7 fusion.4
  80.4 0.3 fusion.50
  80.7 0.3 fusion.21
  81.0 4.5 %collective-permute-start.10 = (f32[1,2,4,64]{3,2,1,0:T(4,128)S(1)}, f32[1,2,4,64]{3,2,1,0:T(4,128)S(1)}, u32[]{:S(2)}, u32[]{:S(2)}) collective-permute-start(f32[1,2,4,64]{3,2,1,0:T(4,128)S(1)} %collective-permute-done.8), channel_id=1, source_target_pairs={{0,15},{1,0},{2,1},{3,2},{4,3},{5,4},{6,5},{7,6},{8,7},{9,8},{10,9... | collective-permute-start | bytes 6152 | tf_op jit(solution)/shard_map/ppermute | solution.py:19
  85.5 0.6 collective-permute-done.11
  86.4 0.4 collective-permute-done.10
  86.8 4.4 %collective-permute-start.12 = (f32[1,2,4,64]{3,2,1,0:T(4,128)S(1)}, f32[1,2,4,64]{3,2,1,0:T(4,128)S(1)}, u32[]{:S(2)}, u32[]{:S(2)}) collective-permute-start(f32[1,2,4,64]{3,2,1,0:T(4,128)S(1)} %collective-permute-done.10), channel_id=1, source_target_pairs={{0,15},{1,0},{2,1},{3,2},{4,3},{5,4},{6,5},{7,6},{8,7},{9,8},{10,9... | collective-permute-start | bytes 6152 | tf_op jit(solution)/shard_map/ppermute | solution.py:19
  91.5 0.4 collective-permute-done.13
  92.1 0.4 collective-permute-done.12
  92.6 4.4 %collective-permute-start.14 = (f32[1,2,4,64]{3,2,1,0:T(4,128)S(1)}, f32[1,2,4,64]{3,2,1,0:T(4,128)S(1)}, u32[]{:S(2)}, u32[]{:S(2)}) collective-permute-start(f32[1,2,4,64]{3,2,1,0:T(4,128)S(1)} %collective-permute-done.12), channel_id=1, source_target_pairs={{0,15},{1,0},{2,1},{3,2},{4,3},{5,4},{6,5},{7,6},{8,7},{9,8},{10,9... | collective-permute-start | bytes 6152 | tf_op jit(solution)/shard_map/ppermute | solution.py:19
  97.2 0.4 collective-permute-done.15
  97.9 0.4 collective-permute-done.14
  98.6 4.8 %collective-permute-done.16 = f32[1,2,4,64]{3,2,1,0:T(4,128)S(1)} collective-permute-done((f32[1,2,4,64]{3,2,1,0:T(4,128)S(1)}, f32[1,2,4,64]{3,2,1,0:T(4,128)S(1)}, u32[]{:S(2)}, u32[]{:S(2)}) %collective-permute-start.16) | collective-permute-done | bytes 2080 | tf_op jit(solution)/shard_map/ppermute | solution.py:17
  104.0 36.9 %psum.36 = f32[1,2,4]{2,1,0:T(2,128)S(1)} all-reduce(f32[1,2,4]{2,1,0:T(2,128)S(1)} %maximum_bitcast_fusion.6), channel_id=1, replica_groups=mesh['dom'=2,'blk'=16] {'dom','blk'}, use_global_device_ids=true, to_apply=%region_4.7 | all-reduce | flops 8 | bytes 64 | tf_op jit(solution)/shard_map/psum | solution.py:134
  141.2 41.4 %psum.37 = f32[4]{0:T(128)S(1)} all-reduce(f32[4]{0:T(128)S(1)} %fusion.118), channel_id=1, replica_groups=mesh['dom'=2,'blk'=16] {'dom','blk'}, use_global_device_ids=true, to_apply=%region_6.9 | all-reduce | flops 4 | bytes 32 | tf_op jit(solution)/shard_map/psum | solution.py:137
  182.9 1.3 collective-permute-start.18
  184.2 4.0 %collective-permute-start.19 = (f32[1,2,4,64]{3,2,1,0:T(4,128)S(1)}, f32[1,2,4,64]{3,2,1,0:T(4,128)S(1)}, u32[]{:S(2)}, u32[]{:S(2)}) collective-permute-start(f32[1,2,4,64]{3,2,1,0:T(4,128)S(1)} %fusion.188), channel_id=1, source_target_pairs={{0,15},{1,0},{2,1},{3,2},{4,3},{5,4},{6,5},{7,6},{8,7},{9,8},{10,9... | collective-permute-start | bytes 6152 | tf_op jit(solution)/shard_map/ppermute | solution.py:19
  188.2 4.4 %all_gather.7 = f32[2,4,2,512]{3,1,0,2:T(4,128)S(1)} all-gather(f32[2,4,1,512]{3,1,0,2:T(4,128)S(1)} %get-tuple-element.23), channel_id=1, replica_groups=mesh['dom'=2,'blk'=16] {'dom'}, dimensions={2}, use_global_device_ids=true | all-gather | bytes 49152 | tf_op jit(solution)/shard_map/all_gather | solution.py:92
  192.7 0.6 gather_fusion.3
  193.7 1.3 collective-permute-start.17
  195.0 0.6 copy.92
  195.8 4.4 %collective-permute-start.21 = (f32[1,2,4,64]{3,2,1,0:T(4,128)S(1)}, f32[1,2,4,64]{3,2,1,0:T(4,128)S(1)}, u32[]{:S(2)}, u32[]{:S(2)}) collective-permute-start(f32[1,2,4,64]{3,2,1,0:T(4,128)S(1)} %collective-permute-done.19), channel_id=1, source_target_pairs={{0,15},{1,0},{2,1},{3,2},{4,3},{5,4},{6,5},{7,6},{8,7},{9,8},{10,9... | collective-permute-start | bytes 6152 | tf_op jit(solution)/shard_map/ppermute | solution.py:19
  200.5 0.3 convolution_add_fusion.7
  200.8 5.5 %collective-permute-done.22 = f32[1,2,4,64]{3,2,1,0:T(4,128)S(1)} collective-permute-done((f32[1,2,4,64]{3,2,1,0:T(4,128)S(1)}, f32[1,2,4,64]{3,2,1,0:T(4,128)S(1)}, u32[]{:S(2)}, u32[]{:S(2)}) %collective-permute-start.22) | collective-permute-done | bytes 2080 | tf_op jit(solution)/shard_map/ppermute | solution.py:17
  206.6 4.4 %collective-permute-start.23 = (f32[1,2,4,64]{3,2,1,0:T(4,128)S(1)}, f32[1,2,4,64]{3,2,1,0:T(4,128)S(1)}, u32[]{:S(2)}, u32[]{:S(2)}) collective-permute-start(f32[1,2,4,64]{3,2,1,0:T(4,128)S(1)} %collective-permute-done.21), channel_id=1, source_target_pairs={{0,15},{1,0},{2,1},{3,2},{4,3},{5,4},{6,5},{7,6},{8,7},{9,8},{10,9... | collective-permute-start | bytes 6152 | tf_op jit(solution)/shard_map/ppermute | solution.py:19
  211.3 1.0 collective-permute-done.24
  212.6 4.4 %collective-permute-start.25 = (f32[1,2,4,64]{3,2,1,0:T(4,128)S(1)}, f32[1,2,4,64]{3,2,1,0:T(4,128)S(1)}, u32[]{:S(2)}, u32[]{:S(2)}) collective-permute-start(f32[1,2,4,64]{3,2,1,0:T(4,128)S(1)} %collective-permute-done.23), channel_id=1, source_target_pairs={{0,15},{1,0},{2,1},{3,2},{4,3},{5,4},{6,5},{7,6},{8,7},{9,8},{10,9... | collective-permute-start | bytes 6152 | tf_op jit(solution)/shard_map/ppermute | solution.py:19
  217.3 1.0 collective-permute-done.26
  218.6 4.4 %collective-permute-start.27 = (f32[1,2,4,64]{3,2,1,0:T(4,128)S(1)}, f32[1,2,4,64]{3,2,1,0:T(4,128)S(1)}, u32[]{:S(2)}, u32[]{:S(2)}) collective-permute-start(f32[1,2,4,64]{3,2,1,0:T(4,128)S(1)} %collective-permute-done.25), channel_id=1, source_target_pairs={{0,15},{1,0},{2,1},{3,2},{4,3},{5,4},{6,5},{7,6},{8,7},{9,8},{10,9... | collective-permute-start | bytes 6152 | tf_op jit(solution)/shard_map/ppermute | solution.py:19
  223.4 0.6 gather_fusion.2
  224.1 0.7 fusion.7
  224.8 0.3 fusion.42
  225.1 4.4 %collective-permute-start.29 = (f32[1,2,4,64]{3,2,1,0:T(4,128)S(1)}, f32[1,2,4,64]{3,2,1,0:T(4,128)S(1)}, u32[]{:S(2)}, u32[]{:S(2)}) collective-permute-start(f32[1,2,4,64]{3,2,1,0:T(4,128)S(1)} %collective-permute-done.27), channel_id=1, source_target_pairs={{0,15},{1,0},{2,1},{3,2},{4,3},{5,4},{6,5},{7,6},{8,7},{9,8},{10,9... | collective-permute-start | bytes 6152 | tf_op jit(solution)/shard_map/ppermute | solution.py:19
  229.8 1.0 collective-permute-done.30
  231.1 4.4 %collective-permute-start.31 = (f32[1,2,4,64]{3,2,1,0:T(4,128)S(1)}, f32[1,2,4,64]{3,2,1,0:T(4,128)S(1)}, u32[]{:S(2)}, u32[]{:S(2)}) collective-permute-start(f32[1,2,4,64]{3,2,1,0:T(4,128)S(1)} %collective-permute-done.29), channel_id=1, source_target_pairs={{0,15},{1,0},{2,1},{3,2},{4,3},{5,4},{6,5},{7,6},{8,7},{9,8},{10,9... | collective-permute-start | bytes 6152 | tf_op jit(solution)/shard_map/ppermute | solution.py:19
  235.8 1.0 collective-permute-done.32
  237.2 0.3 fusion.11
  237.5 5.4 %collective-permute-done.33 = f32[1,2,4,64]{3,2,1,0:T(4,128)S(1)} collective-permute-done((f32[1,2,4,64]{3,2,1,0:T(4,128)S(1)}, f32[1,2,4,64]{3,2,1,0:T(4,128)S(1)}, u32[]{:S(2)}, u32[]{:S(2)}) %collective-permute-start.33) | collective-permute-done | bytes 2080 | tf_op jit(solution)/shard_map/ppermute | solution.py:17
  243.6 36.8 %psum.38 = f32[2,2,4]{2,1,0:T(2,128)S(1)} all-reduce(f32[2,2,4]{2,1,0:T(2,128)S(1)} %pad_maximum_fusion.6), channel_id=1, replica_groups=mesh['dom'=2,'blk'=16] {'dom','blk'}, use_global_device_ids=true, to_apply=%region_11.14 | all-reduce | flops 16 | bytes 128 | tf_op jit(solution)/shard_map/psum | solution.py:134
  280.8 42.2 %psum.39 = f32[4]{0:T(128)S(1)} all-reduce(f32[4]{0:T(128)S(1)} %fusion.114), channel_id=1, replica_groups=mesh['dom'=2,'blk'=16] {'dom','blk'}, use_global_device_ids=true, to_apply=%region_13.16 | all-reduce | flops 4 | bytes 32 | tf_op jit(solution)/shard_map/psum | solution.py:137
  323.6 0.6 copy.93
  324.2 0.7 stack.135
  (137 shorter events, 10.6 us)
Async XLA Ops:
  0.6 79.1 %copy-start = (bf16[1,2,4,2,256,256]{5,4,3,2,1,0:T(8,128)(2,1)S(1)}, bf16[1,2,4,2,256,256]{5,4,3,2,1,0:T(8,128)(2,1)}, u32[]{:S(2)}) copy-start(bf16[1,2,4,2,256,256]{5,4,3,2,1,0:T(8,128)(2,1)} %param.13) | copy-start | bytes 6291460
  45.5 17.0 %collective-permute-start.2 = (f32[1,2,4,64]{3,2,1,0:T(4,128)S(1)}, f32[1,2,4,64]{3,2,1,0:T(4,128)S(1)}, u32[]{:S(2)}, u32[]{:S(2)}) collective-permute-start(f32[1,2,4,64]{3,2,1,0:T(4,128)S(1)} %fusion.189), channel_id=1, source_target_pairs={{0,15},{1,0},{2,1},{3,2},{4,3},{5,4},{6,5},{7,6},{8,7},{9,8},{10,9... | collective-permute-start | bytes 6152 | tf_op jit(solution)/shard_map/ppermute | solution.py:19
  47.2 15.2 %collective-permute-start.3 = (f32[1,2,4,64]{3,2,1,0:T(4,128)S(1)}, f32[1,2,4,64]{3,2,1,0:T(4,128)S(1)}, u32[]{:S(2)}, u32[]{:S(2)}) collective-permute-start(f32[1,2,4,64]{3,2,1,0:T(4,128)S(1)} %fusion.189), channel_id=1, source_target_pairs={{0,1},{1,2},{2,3},{3,4},{4,5},{5,6},{6,7},{7,8},{8,9},{9,10},{10,1... | collective-permute-start | bytes 6152 | tf_op jit(solution)/shard_map/ppermute | solution.py:17
  47.2 31.8 %collective-permute-start = (bf16[2,4,1,512]{3,1,0,2:T(4,128)(2,1)S(1)}, bf16[2,4,1,512]{3,1,0,2:T(4,128)(2,1)S(1)}, u32[]{:S(2)}, u32[]{:S(2)}) collective-permute-start(bf16[2,4,1,512]{3,1,0,2:T(4,128)(2,1)S(1)} %get-tuple-element.24), channel_id=1, source_target_pairs={{0,1},{1,2},{2,3},{3,4},{4,5},{5,6},{6,7},{7,8},{8,9},{9,10},{10,1... | collective-permute-start | bytes 24584 | tf_op jit(solution)/shard_map/ppermute | solution.py:33
  50.0 29.0 %collective-permute-start.1 = (bf16[2,4,1,512]{3,1,0,2:T(4,128)(2,1)S(1)}, bf16[2,4,1,512]{3,1,0,2:T(4,128)(2,1)S(1)}, u32[]{:S(2)}, u32[]{:S(2)}) collective-permute-start(bf16[2,4,1,512]{3,1,0,2:T(4,128)(2,1)S(1)} %get-tuple-element.24), channel_id=1, source_target_pairs={{1,0},{2,1},{3,2},{4,3},{5,4},{6,5},{7,6},{8,7},{9,8},{10,9},{11,1... | collective-permute-start | bytes 24584 | tf_op jit(solution)/shard_map/ppermute | solution.py:35
  61.3 42.4 %copy-start.2 = (bf16[1,2,64,512]{3,2,1,0:T(8,128)(2,1)S(1)}, bf16[1,2,64,512]{3,2,1,0:T(8,128)(2,1)}, u32[]{:S(2)}) copy-start(bf16[1,2,64,512]{3,2,1,0:T(8,128)(2,1)} %param.17) | copy-start | bytes 393220
  62.4 5.8 %collective-permute-start.5 = (f32[1,2,4,64]{3,2,1,0:T(4,128)S(1)}, f32[1,2,4,64]{3,2,1,0:T(4,128)S(1)}, u32[]{:S(2)}, u32[]{:S(2)}) collective-permute-start(f32[1,2,4,64]{3,2,1,0:T(4,128)S(1)} %collective-permute-done.3), channel_id=1, source_target_pairs={{0,1},{1,2},{2,3},{3,4},{4,5},{5,6},{6,7},{7,8},{8,9},{9,10},{10,1... | collective-permute-start | bytes 6152 | tf_op jit(solution)/shard_map/ppermute | solution.py:17
  62.6 5.9 %collective-permute-start.4 = (f32[1,2,4,64]{3,2,1,0:T(4,128)S(1)}, f32[1,2,4,64]{3,2,1,0:T(4,128)S(1)}, u32[]{:S(2)}, u32[]{:S(2)}) collective-permute-start(f32[1,2,4,64]{3,2,1,0:T(4,128)S(1)} %collective-permute-done.2), channel_id=1, source_target_pairs={{0,15},{1,0},{2,1},{3,2},{4,3},{5,4},{6,5},{7,6},{8,7},{9,8},{10,9... | collective-permute-start | bytes 6152 | tf_op jit(solution)/shard_map/ppermute | solution.py:19
  67.1 115.6 %copy-start.1 = (bf16[1,2,64,512]{3,2,1,0:T(8,128)(2,1)S(1)}, bf16[1,2,64,512]{3,2,1,0:T(8,128)(2,1)}, u32[]{:S(2)}) copy-start(bf16[1,2,64,512]{3,2,1,0:T(8,128)(2,1)} %param.16) | copy-start | bytes 393220
  68.2 5.7 %collective-permute-start.7 = (f32[1,2,4,64]{3,2,1,0:T(4,128)S(1)}, f32[1,2,4,64]{3,2,1,0:T(4,128)S(1)}, u32[]{:S(2)}, u32[]{:S(2)}) collective-permute-start(f32[1,2,4,64]{3,2,1,0:T(4,128)S(1)} %collective-permute-done.5), channel_id=1, source_target_pairs={{0,1},{1,2},{2,3},{3,4},{4,5},{5,6},{6,7},{7,8},{8,9},{9,10},{10,1... | collective-permute-start | bytes 6152 | tf_op jit(solution)/shard_map/ppermute | solution.py:17
  68.5 5.8 %collective-permute-start.6 = (f32[1,2,4,64]{3,2,1,0:T(4,128)S(1)}, f32[1,2,4,64]{3,2,1,0:T(4,128)S(1)}, u32[]{:S(2)}, u32[]{:S(2)}) collective-permute-start(f32[1,2,4,64]{3,2,1,0:T(4,128)S(1)} %collective-permute-done.4), channel_id=1, source_target_pairs={{0,15},{1,0},{2,1},{3,2},{4,3},{5,4},{6,5},{7,6},{8,7},{9,8},{10,9... | collective-permute-start | bytes 6152 | tf_op jit(solution)/shard_map/ppermute | solution.py:19
  73.9 6.5 %collective-permute-start.9 = (f32[1,2,4,64]{3,2,1,0:T(4,128)S(1)}, f32[1,2,4,64]{3,2,1,0:T(4,128)S(1)}, u32[]{:S(2)}, u32[]{:S(2)}) collective-permute-start(f32[1,2,4,64]{3,2,1,0:T(4,128)S(1)} %collective-permute-done.7), channel_id=1, source_target_pairs={{0,1},{1,2},{2,3},{3,4},{4,5},{5,6},{6,7},{7,8},{8,9},{9,10},{10,1... | collective-permute-start | bytes 6152 | tf_op jit(solution)/shard_map/ppermute | solution.py:17
  74.3 6.4 %collective-permute-start.8 = (f32[1,2,4,64]{3,2,1,0:T(4,128)S(1)}, f32[1,2,4,64]{3,2,1,0:T(4,128)S(1)}, u32[]{:S(2)}, u32[]{:S(2)}) collective-permute-start(f32[1,2,4,64]{3,2,1,0:T(4,128)S(1)} %collective-permute-done.6), channel_id=1, source_target_pairs={{0,15},{1,0},{2,1},{3,2},{4,3},{5,4},{6,5},{7,6},{8,7},{9,8},{10,9... | collective-permute-start | bytes 6152 | tf_op jit(solution)/shard_map/ppermute | solution.py:19
  80.4 5.8 %collective-permute-start.11 = (f32[1,2,4,64]{3,2,1,0:T(4,128)S(1)}, f32[1,2,4,64]{3,2,1,0:T(4,128)S(1)}, u32[]{:S(2)}, u32[]{:S(2)}) collective-permute-start(f32[1,2,4,64]{3,2,1,0:T(4,128)S(1)} %collective-permute-done.9), channel_id=1, source_target_pairs={{0,1},{1,2},{2,3},{3,4},{4,5},{5,6},{6,7},{7,8},{8,9},{9,10},{10,1... | collective-permute-start | bytes 6152 | tf_op jit(solution)/shard_map/ppermute | solution.py:17
  81.0 5.8 %collective-permute-start.10 = (f32[1,2,4,64]{3,2,1,0:T(4,128)S(1)}, f32[1,2,4,64]{3,2,1,0:T(4,128)S(1)}, u32[]{:S(2)}, u32[]{:S(2)}) collective-permute-start(f32[1,2,4,64]{3,2,1,0:T(4,128)S(1)} %collective-permute-done.8), channel_id=1, source_target_pairs={{0,15},{1,0},{2,1},{3,2},{4,3},{5,4},{6,5},{7,6},{8,7},{9,8},{10,9... | collective-permute-start | bytes 6152 | tf_op jit(solution)/shard_map/ppermute | solution.py:19
  86.2 5.7 %collective-permute-start.13 = (f32[1,2,4,64]{3,2,1,0:T(4,128)S(1)}, f32[1,2,4,64]{3,2,1,0:T(4,128)S(1)}, u32[]{:S(2)}, u32[]{:S(2)}) collective-permute-start(f32[1,2,4,64]{3,2,1,0:T(4,128)S(1)} %collective-permute-done.11), channel_id=1, source_target_pairs={{0,1},{1,2},{2,3},{3,4},{4,5},{5,6},{6,7},{7,8},{8,9},{9,10},{10,1... | collective-permute-start | bytes 6152 | tf_op jit(solution)/shard_map/ppermute | solution.py:17
  86.8 5.7 %collective-permute-start.12 = (f32[1,2,4,64]{3,2,1,0:T(4,128)S(1)}, f32[1,2,4,64]{3,2,1,0:T(4,128)S(1)}, u32[]{:S(2)}, u32[]{:S(2)}) collective-permute-start(f32[1,2,4,64]{3,2,1,0:T(4,128)S(1)} %collective-permute-done.10), channel_id=1, source_target_pairs={{0,15},{1,0},{2,1},{3,2},{4,3},{5,4},{6,5},{7,6},{8,7},{9,8},{10,9... | collective-permute-start | bytes 6152 | tf_op jit(solution)/shard_map/ppermute | solution.py:19
  91.9 5.7 %collective-permute-start.15 = (f32[1,2,4,64]{3,2,1,0:T(4,128)S(1)}, f32[1,2,4,64]{3,2,1,0:T(4,128)S(1)}, u32[]{:S(2)}, u32[]{:S(2)}) collective-permute-start(f32[1,2,4,64]{3,2,1,0:T(4,128)S(1)} %collective-permute-done.13), channel_id=1, source_target_pairs={{0,1},{1,2},{2,3},{3,4},{4,5},{5,6},{6,7},{7,8},{8,9},{9,10},{10,1... | collective-permute-start | bytes 6152 | tf_op jit(solution)/shard_map/ppermute | solution.py:17
  92.6 5.7 %collective-permute-start.14 = (f32[1,2,4,64]{3,2,1,0:T(4,128)S(1)}, f32[1,2,4,64]{3,2,1,0:T(4,128)S(1)}, u32[]{:S(2)}, u32[]{:S(2)}) collective-permute-start(f32[1,2,4,64]{3,2,1,0:T(4,128)S(1)} %collective-permute-done.12), channel_id=1, source_target_pairs={{0,15},{1,0},{2,1},{3,2},{4,3},{5,4},{6,5},{7,6},{8,7},{9,8},{10,9... | collective-permute-start | bytes 6152 | tf_op jit(solution)/shard_map/ppermute | solution.py:19
  97.6 5.7 %collective-permute-start.16 = (f32[1,2,4,64]{3,2,1,0:T(4,128)S(1)}, f32[1,2,4,64]{3,2,1,0:T(4,128)S(1)}, u32[]{:S(2)}, u32[]{:S(2)}) collective-permute-start(f32[1,2,4,64]{3,2,1,0:T(4,128)S(1)} %collective-permute-done.15), channel_id=1, source_target_pairs={{0,1},{1,2},{2,3},{3,4},{4,5},{5,6},{6,7},{7,8},{8,9},{9,10},{10,1... | collective-permute-start | bytes 6152 | tf_op jit(solution)/shard_map/ppermute | solution.py:17
  182.9 40.5 %collective-permute-start.18 = (bf16[2,4,1,512]{3,1,0,2:T(4,128)(2,1)S(1)}, bf16[2,4,1,512]{3,1,0,2:T(4,128)(2,1)S(1)}, u32[]{:S(2)}, u32[]{:S(2)}) collective-permute-start(bf16[2,4,1,512]{3,1,0,2:T(4,128)(2,1)S(1)} %get-tuple-element.22), channel_id=1, source_target_pairs={{1,0},{2,1},{3,2},{4,3},{5,4},{6,5},{7,6},{8,7},{9,8},{10,9},{11,1... | collective-permute-start | bytes 24584 | tf_op jit(solution)/shard_map/ppermute | solution.py:35
  184.2 11.6 %collective-permute-start.19 = (f32[1,2,4,64]{3,2,1,0:T(4,128)S(1)}, f32[1,2,4,64]{3,2,1,0:T(4,128)S(1)}, u32[]{:S(2)}, u32[]{:S(2)}) collective-permute-start(f32[1,2,4,64]{3,2,1,0:T(4,128)S(1)} %fusion.188), channel_id=1, source_target_pairs={{0,15},{1,0},{2,1},{3,2},{4,3},{5,4},{6,5},{7,6},{8,7},{9,8},{10,9... | collective-permute-start | bytes 6152 | tf_op jit(solution)/shard_map/ppermute | solution.py:19
  193.6 6.8 %collective-permute-start.20 = (f32[1,2,4,64]{3,2,1,0:T(4,128)S(1)}, f32[1,2,4,64]{3,2,1,0:T(4,128)S(1)}, u32[]{:S(2)}, u32[]{:S(2)}) collective-permute-start(f32[1,2,4,64]{3,2,1,0:T(4,128)S(1)} %fusion.188), channel_id=1, source_target_pairs={{0,1},{1,2},{2,3},{3,4},{4,5},{5,6},{6,7},{7,8},{8,9},{9,10},{10,1... | collective-permute-start | bytes 6152 | tf_op jit(solution)/shard_map/ppermute | solution.py:17
  193.7 29.6 %collective-permute-start.17 = (bf16[2,4,1,512]{3,1,0,2:T(4,128)(2,1)S(1)}, bf16[2,4,1,512]{3,1,0,2:T(4,128)(2,1)S(1)}, u32[]{:S(2)}, u32[]{:S(2)}) collective-permute-start(bf16[2,4,1,512]{3,1,0,2:T(4,128)(2,1)S(1)} %get-tuple-element.22), channel_id=1, source_target_pairs={{0,1},{1,2},{2,3},{3,4},{4,5},{5,6},{6,7},{7,8},{8,9},{9,10},{10,1... | collective-permute-start | bytes 24584 | tf_op jit(solution)/shard_map/ppermute | solution.py:33
  195.8 10.8 %collective-permute-start.21 = (f32[1,2,4,64]{3,2,1,0:T(4,128)S(1)}, f32[1,2,4,64]{3,2,1,0:T(4,128)S(1)}, u32[]{:S(2)}, u32[]{:S(2)}) collective-permute-start(f32[1,2,4,64]{3,2,1,0:T(4,128)S(1)} %collective-permute-done.19), channel_id=1, source_target_pairs={{0,15},{1,0},{2,1},{3,2},{4,3},{5,4},{6,5},{7,6},{8,7},{9,8},{10,9... | collective-permute-start | bytes 6152 | tf_op jit(solution)/shard_map/ppermute | solution.py:19
  200.5 5.8 %collective-permute-start.22 = (f32[1,2,4,64]{3,2,1,0:T(4,128)S(1)}, f32[1,2,4,64]{3,2,1,0:T(4,128)S(1)}, u32[]{:S(2)}, u32[]{:S(2)}) collective-permute-start(f32[1,2,4,64]{3,2,1,0:T(4,128)S(1)} %collective-permute-done.20), channel_id=1, source_target_pairs={{0,1},{1,2},{2,3},{3,4},{4,5},{5,6},{6,7},{7,8},{8,9},{9,10},{10,1... | collective-permute-start | bytes 6152 | tf_op jit(solution)/shard_map/ppermute | solution.py:17
  206.5 5.8 %collective-permute-start.24 = (f32[1,2,4,64]{3,2,1,0:T(4,128)S(1)}, f32[1,2,4,64]{3,2,1,0:T(4,128)S(1)}, u32[]{:S(2)}, u32[]{:S(2)}) collective-permute-start(f32[1,2,4,64]{3,2,1,0:T(4,128)S(1)} %collective-permute-done.22), channel_id=1, source_target_pairs={{0,1},{1,2},{2,3},{3,4},{4,5},{5,6},{6,7},{7,8},{8,9},{9,10},{10,1... | collective-permute-start | bytes 6152 | tf_op jit(solution)/shard_map/ppermute | solution.py:17
  206.6 6.0 %collective-permute-start.23 = (f32[1,2,4,64]{3,2,1,0:T(4,128)S(1)}, f32[1,2,4,64]{3,2,1,0:T(4,128)S(1)}, u32[]{:S(2)}, u32[]{:S(2)}) collective-permute-start(f32[1,2,4,64]{3,2,1,0:T(4,128)S(1)} %collective-permute-done.21), channel_id=1, source_target_pairs={{0,15},{1,0},{2,1},{3,2},{4,3},{5,4},{6,5},{7,6},{8,7},{9,8},{10,9... | collective-permute-start | bytes 6152 | tf_op jit(solution)/shard_map/ppermute | solution.py:19
  212.5 5.8 %collective-permute-start.26 = (f32[1,2,4,64]{3,2,1,0:T(4,128)S(1)}, f32[1,2,4,64]{3,2,1,0:T(4,128)S(1)}, u32[]{:S(2)}, u32[]{:S(2)}) collective-permute-start(f32[1,2,4,64]{3,2,1,0:T(4,128)S(1)} %collective-permute-done.24), channel_id=1, source_target_pairs={{0,1},{1,2},{2,3},{3,4},{4,5},{5,6},{6,7},{7,8},{8,9},{9,10},{10,1... | collective-permute-start | bytes 6152 | tf_op jit(solution)/shard_map/ppermute | solution.py:17
  212.6 6.0 %collective-permute-start.25 = (f32[1,2,4,64]{3,2,1,0:T(4,128)S(1)}, f32[1,2,4,64]{3,2,1,0:T(4,128)S(1)}, u32[]{:S(2)}, u32[]{:S(2)}) collective-permute-start(f32[1,2,4,64]{3,2,1,0:T(4,128)S(1)} %collective-permute-done.23), channel_id=1, source_target_pairs={{0,15},{1,0},{2,1},{3,2},{4,3},{5,4},{6,5},{7,6},{8,7},{9,8},{10,9... | collective-permute-start | bytes 6152 | tf_op jit(solution)/shard_map/ppermute | solution.py:19
  218.6 6.2 %collective-permute-start.28 = (f32[1,2,4,64]{3,2,1,0:T(4,128)S(1)}, f32[1,2,4,64]{3,2,1,0:T(4,128)S(1)}, u32[]{:S(2)}, u32[]{:S(2)}) collective-permute-start(f32[1,2,4,64]{3,2,1,0:T(4,128)S(1)} %collective-permute-done.26), channel_id=1, source_target_pairs={{0,1},{1,2},{2,3},{3,4},{4,5},{5,6},{6,7},{7,8},{8,9},{9,10},{10,1... | collective-permute-start | bytes 6152 | tf_op jit(solution)/shard_map/ppermute | solution.py:17
  218.6 6.4 %collective-permute-start.27 = (f32[1,2,4,64]{3,2,1,0:T(4,128)S(1)}, f32[1,2,4,64]{3,2,1,0:T(4,128)S(1)}, u32[]{:S(2)}, u32[]{:S(2)}) collective-permute-start(f32[1,2,4,64]{3,2,1,0:T(4,128)S(1)} %collective-permute-done.25), channel_id=1, source_target_pairs={{0,15},{1,0},{2,1},{3,2},{4,3},{5,4},{6,5},{7,6},{8,7},{9,8},{10,9... | collective-permute-start | bytes 6152 | tf_op jit(solution)/shard_map/ppermute | solution.py:19
  225.0 5.8 %collective-permute-start.30 = (f32[1,2,4,64]{3,2,1,0:T(4,128)S(1)}, f32[1,2,4,64]{3,2,1,0:T(4,128)S(1)}, u32[]{:S(2)}, u32[]{:S(2)}) collective-permute-start(f32[1,2,4,64]{3,2,1,0:T(4,128)S(1)} %collective-permute-done.28), channel_id=1, source_target_pairs={{0,1},{1,2},{2,3},{3,4},{4,5},{5,6},{6,7},{7,8},{8,9},{9,10},{10,1... | collective-permute-start | bytes 6152 | tf_op jit(solution)/shard_map/ppermute | solution.py:17
  225.1 6.0 %collective-permute-start.29 = (f32[1,2,4,64]{3,2,1,0:T(4,128)S(1)}, f32[1,2,4,64]{3,2,1,0:T(4,128)S(1)}, u32[]{:S(2)}, u32[]{:S(2)}) collective-permute-start(f32[1,2,4,64]{3,2,1,0:T(4,128)S(1)} %collective-permute-done.27), channel_id=1, source_target_pairs={{0,15},{1,0},{2,1},{3,2},{4,3},{5,4},{6,5},{7,6},{8,7},{9,8},{10,9... | collective-permute-start | bytes 6152 | tf_op jit(solution)/shard_map/ppermute | solution.py:19
  231.1 5.8 %collective-permute-start.32 = (f32[1,2,4,64]{3,2,1,0:T(4,128)S(1)}, f32[1,2,4,64]{3,2,1,0:T(4,128)S(1)}, u32[]{:S(2)}, u32[]{:S(2)}) collective-permute-start(f32[1,2,4,64]{3,2,1,0:T(4,128)S(1)} %collective-permute-done.30), channel_id=1, source_target_pairs={{0,1},{1,2},{2,3},{3,4},{4,5},{5,6},{6,7},{7,8},{8,9},{9,10},{10,1... | collective-permute-start | bytes 6152 | tf_op jit(solution)/shard_map/ppermute | solution.py:17
  231.1 6.0 %collective-permute-start.31 = (f32[1,2,4,64]{3,2,1,0:T(4,128)S(1)}, f32[1,2,4,64]{3,2,1,0:T(4,128)S(1)}, u32[]{:S(2)}, u32[]{:S(2)}) collective-permute-start(f32[1,2,4,64]{3,2,1,0:T(4,128)S(1)} %collective-permute-done.29), channel_id=1, source_target_pairs={{0,15},{1,0},{2,1},{3,2},{4,3},{5,4},{6,5},{7,6},{8,7},{9,8},{10,9... | collective-permute-start | bytes 6152 | tf_op jit(solution)/shard_map/ppermute | solution.py:19
  237.1 5.8 %collective-permute-start.33 = (f32[1,2,4,64]{3,2,1,0:T(4,128)S(1)}, f32[1,2,4,64]{3,2,1,0:T(4,128)S(1)}, u32[]{:S(2)}, u32[]{:S(2)}) collective-permute-start(f32[1,2,4,64]{3,2,1,0:T(4,128)S(1)} %collective-permute-done.32), channel_id=1, source_target_pairs={{0,1},{1,2},{2,3},{3,4},{4,5},{5,6},{6,7},{7,8},{8,9},{9,10},{10,1... | collective-permute-start | bytes 6152 | tf_op jit(solution)/shard_map/ppermute | solution.py:17
